TPU v7x, 512 devices: a whole 4x4x16 slice. The times are simulated.
512 devices in a mesh: seq: 8 (over x, core), tp: 16 (over z), req: 4 (over y).
Axes of the slice: x: 4, y: 4, z: 16, core: 2. Of those that a mesh axis runs over, the one named last changes fastest.
Arguments:
- tokens: bfloat16 [32768, 1792], P(('req', 'seq'), 'tp'), parts along dimension 0, may hold values from -6 to 6
- w_in: bfloat16 [1792, 4096], P(None, 'tp'), may hold values from -0.125 to 0.125
- conv_w: float32 [3, 1792], P(None, 'tp'), may hold values from -3 to 3
- head_gain: float32 [1792], P('tp'), may hold values from 0.1 to 1.9
- w_out: bfloat16 [1792, 1792], P('tp'), may hold values from -0.125 to 0.125
- prompt_lens: int32 [16], P('req'), parts along dimension 0, may hold values from 1 to 4096, 8192 in all
- req_group: int32 [128], P('req'), parts along dimension 0, may hold values from 0 to 3, as said below
- row_request: int32 [128], P('req'), parts along dimension 0, may hold values from 0 to 31, each once
Outputs:
- mixed: bfloat16 [32768, 1792], P(('req', 'seq'), 'tp'), parts along dimension 0
- req_state: float32 [128, 16, 273, 112], P(('req', 'seq'), 'tp'), parts along dimension 0
- req_norm: float32 [128, 16, 273], P(('req', 'seq'), 'tp'), parts along dimension 0
- req_edge: bfloat16 [128, 2, 1792], P(('req', 'seq'), None, 'tp'), parts along dimension 0
There are 4 independent parts, one for each index of `req`. A program takes and returns all parts, laid end to end along the dimension named above; an argument that names none is the same for every part. Nothing has to cross between parts.
Inputs may be any that keep to these rules, and one draw needn't show every extreme that they name: `prompt_lens`: the lengths sum to 8192, and the largest is half of 8192. `req_group`: every one of the 4 prompts is shared by at least one request. `row_request`: each request appears once; rows i * 4 to (i + 1) * 4 - 1 lie on index i of seq.
All inputs are finite; a program needn't handle non-finite values.
Results may differ from a plain program's by a relative error of at most 0.019.
Values may be sent and summed in bfloat16 or wider, within the bound.
No kernel may reach another device: no remote copies, remote signals or barrier semaphores. Data moves between devices by JAX's collectives and lax.ppermute only.
A program may use at most 64 MiB of HBM per device.

v0:
```python
import jax
import jax.numpy as jnp
from jax import lax
from jax.sharding import PartitionSpec as P

FEAT = 16
HD = 112
KW = 3
PROMPTS = 4
SLOTS = 4
EPS = 1e-05
HIGH = lax.Precision.HIGHEST


def passed_along(shard, axis, by):
    size = lax.axis_size(axis)
    pairs = [(i, i + by) for i in range(size) if 0 <= i + by < size]
    return lax.ppermute(shard, axis, pairs)


def psum_doubling(parts, axis):
    size = lax.axis_size(axis)
    total = [p.astype(jnp.float32) for p in parts]
    step = 1
    while step < size:
        pairs = [(i, i ^ step) for i in range(size)]
        got = lax.ppermute(tuple((t.astype(jnp.bfloat16) for t in total)), axis, pairs)
        total = [t + g.astype(jnp.float32) for t, g in zip(total, got)]
        step *= 2
    return total


def tail_prefix(tail, tail_seg, axis):
    size, here = (lax.axis_size(axis), lax.axis_index(axis))
    seg_before = tail_seg[jnp.maximum(here - 1, 0)]
    group = tail.astype(jnp.float32)
    before = jnp.zeros_like(group)
    step = 1
    while step < size:
        pairs = [(i, i ^ step) for i in range(size)]
        got = lax.ppermute(group.astype(jnp.bfloat16), axis, pairs).astype(jnp.float32)
        other = here ^ step
        my_end = here | step - 1
        other_end = other | step - 1
        same = (tail_seg[my_end] == tail_seg[other_end]).astype(jnp.float32)
        earlier = other < here
        take = (earlier & (tail_seg[other_end] == seg_before)).astype(jnp.float32)
        before = before + take * got
        group = jnp.where(earlier, group + same * got, got + same * group)
        step *= 2
    return before


def taylor_map(values):
    size = values.shape[-1]
    ones = jnp.ones(values.shape[:-1] + (1,), jnp.float32)
    pairs = (values[..., :, None] * values[..., None, :]).reshape(
        values.shape[:-1] + (size * size,)
    )
    return jnp.concatenate([ones, values, pairs * 0.5**0.5], axis=-1)


def segment_ids(positions, ends):
    return jnp.sum((positions[:, None] >= ends[None, :]).astype(jnp.int32), axis=1)


def local(tokens, w_in, conv_w, head_gain, w_out, prompt_lens, req_group, row_request):
    tok_rows = tokens.shape[0]
    width = 2 * FEAT + 2 * HD
    local_heads = w_in.shape[1] // width
    local_cols = local_heads * HD
    seq_pos = lax.axis_index("seq")
    first_row = seq_pos * tok_rows
    ends = jnp.cumsum(prompt_lens)
    starts = ends - prompt_lens
    positions = first_row + jnp.arange(tok_rows, dtype=jnp.int32)
    seg = segment_ids(positions, ends)
    proj = jnp.dot(
        lax.all_gather(tokens, "tp", axis=1, tiled=True), w_in, preferred_element_type=jnp.float32
    )
    proj = proj.astype(jnp.bfloat16).reshape(tok_rows, local_heads, width)
    gate_pre = proj[:, :, 2 * FEAT + HD :].reshape(tok_rows, local_cols)
    rim = passed_along(gate_pre[tok_rows - (KW - 1) :], "seq", 1)
    extended = jnp.concatenate([rim, gate_pre], 0)
    ext_pos = first_row - (KW - 1) + jnp.arange(tok_rows + KW - 1, dtype=jnp.int32)
    ext_seg = segment_ids(ext_pos, ends)
    gate = jnp.zeros((tok_rows, local_cols), jnp.float32)
    for tap in range(KW):
        low = KW - 1 - tap
        same = (ext_seg[low : low + tok_rows] == seg).astype(jnp.float32)
        gate = (
            gate
            + conv_w[tap][None, :]
            * extended[low : low + tok_rows].astype(jnp.float32)
            * same[:, None]
        )
    qs_b = proj[:, :, :FEAT] * jnp.bfloat16(FEAT ** (-0.25))
    ks_b = proj[:, :, FEAT : 2 * FEAT] * jnp.bfloat16(FEAT ** (-0.25))
    qs = qs_b.astype(jnp.float32)
    ks = ks_b.astype(jnp.float32)
    values = proj[:, :, 2 * FEAT : 2 * FEAT + HD]
    values_f = values.astype(jnp.float32)
    dots = jnp.einsum("thf,shf->hts", qs_b, ks_b, preferred_element_type=jnp.float32)
    visible = (positions[None, :] <= positions[:, None]) & (seg[:, None] == seg[None, :])
    weights = jnp.where(visible[None], 1.0 + dots + 0.5 * dots * dots, 0.0)
    numer = jnp.einsum(
        "hts,shd->thd", weights.astype(jnp.bfloat16), values, preferred_element_type=jnp.float32
    )
    phi_q = taylor_map(qs)
    phi_k = taylor_map(ks)
    fmap = phi_k.shape[-1]
    prompt_index = jnp.arange(PROMPTS, dtype=jnp.int32)
    onehot = (seg[:, None] == prompt_index[None, :]).astype(jnp.float32)
    keyed = (onehot[:, :, None, None] * phi_k[:, None, :, :]).reshape(
        tok_rows, PROMPTS * local_heads * fmap
    )
    contrib_state = lax.dot_general(
        keyed.reshape(tok_rows, PROMPTS, local_heads, fmap),
        values_f,
        (((0,), (0,)), ((2,), (1,))),
        precision=HIGH,
    )
    contrib_norm = jnp.einsum("tg,thf->ghf", onehot, phi_k, precision=HIGH)
    offsets = jnp.arange(KW - 1, dtype=jnp.int32)
    edge_rows = ends[:, None] - (KW - 1) + offsets[None, :]
    edge_valid = edge_rows >= starts[:, None]
    match = ((positions[:, None, None] == edge_rows[None]) & edge_valid[None]).astype(jnp.bfloat16)
    contrib_edge = jnp.einsum("tgj,tc->gjc", match, gate_pre, preferred_element_type=jnp.float32)
    block_ends = (jnp.arange(lax.axis_size("seq"), dtype=jnp.int32) + 1) * tok_rows - 1
    tail_seg = segment_ids(block_ends, ends)
    seg_last = tail_seg[seq_pos]
    in_tail = (seg == seg_last).astype(jnp.float32)
    tail_state = jnp.einsum(
        "thf,thd->hfd", phi_k * in_tail[:, None, None], values_f, precision=HIGH
    )
    seg_before = jnp.sum((first_row - 1 >= ends).astype(jnp.int32))
    tails = lax.all_gather(tail_state.astype(jnp.bfloat16), "seq").astype(jnp.float32)
    block_index = jnp.arange(lax.axis_size("seq"), dtype=jnp.int32)
    chained = ((block_index < seq_pos) & (tail_seg == seg_before)).astype(jnp.float32)
    carry_state = jnp.sum(chained.reshape((-1,) + (1,) * (tails.ndim - 1)) * tails, axis=0)
    carried = ((seg == seg_before) & (first_row > 0)).astype(jnp.float32)
    attended = (
        numer
        + jnp.einsum("thf,hfd->thd", phi_q, carry_state, precision=HIGH) * carried[:, None, None]
    )
    inv_rms = lax.rsqrt(jnp.mean(attended * attended, axis=2, keepdims=True) + EPS)
    gain = head_gain.reshape(local_heads, HD)
    hidden = (
        attended * inv_rms * gain[None] * jax.nn.silu(gate.reshape(tok_rows, local_heads, HD))
    ).astype(jnp.bfloat16)
    hidden = hidden.reshape(tok_rows, local_cols)
    product = jnp.einsum(
        "tk,kgc->gtc",
        hidden,
        w_out.reshape(local_cols, lax.axis_size("tp"), -1),
        preferred_element_type=jnp.bfloat16,
    )
    summed = lax.psum_scatter(product, "tp", scatter_dimension=0, tiled=True)
    mixed = summed.reshape(tok_rows, -1)
    all_state, all_norm, all_edge = psum_doubling(
        (contrib_state, contrib_norm, contrib_edge), "seq"
    )
    scale = lax.rsqrt(prompt_lens.astype(jnp.float32))
    my_requests = lax.dynamic_slice_in_dim(row_request, seq_pos * SLOTS, SLOTS)
    my_groups = jnp.take(req_group, my_requests)
    my_scale = jnp.take(scale, my_groups)
    req_state = (
        jnp.take(all_state, my_groups, axis=1).transpose(1, 0, 2, 3) * my_scale[:, None, None, None]
    )
    req_norm = jnp.take(all_norm, my_groups, axis=0) * my_scale[:, None, None]
    req_edge = jnp.take(all_edge, my_groups, axis=0).astype(jnp.bfloat16)
    return (mixed, req_state, req_norm, req_edge)


def solution(mesh):
    in_specs = (
        P(("req", "seq"), "tp"),
        P(None, "tp"),
        P(None, "tp"),
        P("tp"),
        P("tp", None),
        P("req"),
        P("req"),
        P("req"),
    )
    out_specs = (
        P(("req", "seq"), "tp"),
        P(("req", "seq"), "tp", None, None),
        P(("req", "seq"), "tp", None),
        P(("req", "seq"), None, "tp"),
    )
    return jax.shard_map(local, mesh=mesh, in_specs=in_specs, out_specs=out_specs, check_vma=False)
```

profile of v0, /device:TPU:4, one launch (start us, length us, event | category | flops | bytes accessed | tf_op | source)
XLA Modules:
  0.0 200.5 jit_solution(5603790079659906955)
XLA Ops:
  7.2 0.7 all-gather.4.cloned.1.call-update
  8.0 0.8 reduce-window.7
  8.8 0.1 convert_reduce_fusion.2
  8.9 0.6 dynamic_slice.6
  9.6 0.1 convert_reduce_fusion
  9.7 1.3 bitcast_subtract_fusion
  11.0 0.6 and_convert_fusion.1
  11.6 0.8 slice_bitcast_fusion.4
  12.4 1.4 fusion.74
  13.8 77.7 %all-gather.4.cloned.1.call-done = bf16[1024,1792]{0,1:T(8,128)(2,1)} async-done(((bf16[1024,112]{0,1:T(8,128)(2,1)}), bf16[1024,1792]{0,1:T(8,128)(2,1)}) %all-gather.4.cloned.1.call-update) | async-done | bytes 3670032 | tf_op jit(solution)/shard_map/all_gather | solution.py:79
  91.5 3.2 %fusion.8 = bf16[1024,1,256]{0,2,1:T(8,128)(2,1)S(1)} fusion(bf16[1024,1792]{0,1:T(8,128)(2,1)} %all-gather.4.cloned.1.call-done, bf16[1792,256]{1,0:T(8,128)(2,1)S(1)} %copy-done), kind=kOutput, calls=%fused_computation.15 | convolution fusion | flops 939786240 | bytes 5111808 | tf_op jit(solution)/shard_map/dot_general | solution.py:78
  94.8 1.7 fusion.9
  96.5 1.9 collective-permute-start
  98.4 0.1 multiply_multiply_fusion.1
  98.5 0.1 multiply_multiply_fusion.2
  98.7 0.8 fusion.25
  99.5 12.1 %all-gather.1 = bf16[8,273,112]{2,1,0:T(8,128)(2,1)S(1)} all-gather(bf16[1,273,112]{2,1,0:T(8,128)(2,1)S(1)} %fusion.25), channel_id=2, replica_groups=mesh['seq'=8,'tp'=16,'req'=4] {'seq'}, dimensions={0}, use_global_device_ids=true | all-gather | bytes 550368 | tf_op jit(solution)/shard_map/all_gather | solution.py:137
  111.6 0.2 fusion.21
  111.9 1.2 multiply_reduce_fusion
  113.2 3.2 %fusion.38 = bf16[1024,1792]{0,1} fusion(bf16[112,1792]{1,0:T(8,128)(2,1)S(1)} %copy-done.2, bf16[1024,112]{0,1:T(8,128)(2,1)S(1)} %slice_bitcast_fusion, f32[1,112,1024]{2,1,0:T(8,128)S(1)} %get-tuple-element.39, bf16[2,112]{0,1:T(8,128)(2,1)S(1)} %collective-permute-done, f32[1024]{0:T(1024)S(1)} %get-tuple-element.28, f32[112]{0:T(128)S(1)} %get-tuple-element.33, ...), kind=kOutput, calls=%fused_computation.57 | convolution fusion | flops 413908992 | bytes 4778176
  116.4 0.6 copy-done.4
  117.1 0.6 gather_fusion
  117.8 0.6 gather_fusion.2
  118.5 0.2 fusion.91
  118.7 2.3 %collective-permute-start.7 = (bf16[4,2,112]{2,0,1:T(4,128)(2,1)S(1)}, bf16[4,2,112]{2,0,1:T(4,128)(2,1)S(1)}, u32[]{:S(2)}, u32[]{:S(2)}) collective-permute-start(bf16[4,2,112]{2,0,1:T(4,128)(2,1)S(1)} %get-tuple-element.40), channel_id=1, source_target_pairs={{0,64},{64,0},{128,192},{192,128},{256,320},{320,256},{384,448},{4... | collective-permute-start | bytes 5384 | tf_op jit(solution)/shard_map/ppermute | solution.py:27
  121.0 0.8 fusion.65
  121.8 2.1 %collective-permute-start.4 = (bf16[4,1,273]{2,0,1:T(4,128)(2,1)S(1)}, bf16[4,1,273]{2,0,1:T(4,128)(2,1)S(1)}, u32[]{:S(2)}, u32[]{:S(2)}) collective-permute-start(bf16[4,1,273]{2,0,1:T(4,128)(2,1)S(1)} %convert_bitcast_fusion.3), channel_id=1, source_target_pairs={{0,64},{64,0},{128,192},{192,128},{256,320},{320,256},{384,448},{4... | collective-permute-start | bytes 6560 | tf_op jit(solution)/shard_map/ppermute | solution.py:27
  123.9 0.2 maximum_bitcast_fusion.2
  124.0 2.3 %fusion = f32[4,273,112]{2,1,0:T(8,128)S(1)} fusion(f32[1024,273]{0,1:T(8,128)S(1)} %maximum_bitcast_fusion.2, f32[1024,4]{0,1:T(4,128)S(1)} %fusion.66, bf16[1024,1,256]{0,2,1:T(8,128)(2,1)S(1)} %fusion.8), kind=kOutput, calls=%fused_computation.6 | convolution fusion | flops 1503989760 | bytes 1881856 | tf_op jit(solution)/shard_map/dot_general | solution.py:117
  126.4 2.3 %collective-permute-start.1 = (bf16[1,4,273,112]{3,2,1,0:T(8,128)(2,1)S(1)}, bf16[1,4,273,112]{3,2,1,0:T(8,128)(2,1)S(1)}, u32[]{:S(2)}, u32[]{:S(2)}) collective-permute-start(bf16[1,4,273,112]{3,2,1,0:T(8,128)(2,1)S(1)} %convert_bitcast_fusion), channel_id=1, source_target_pairs={{0,64},{64,0},{128,192},{192,128},{256,320},{320,256},{384,448},{4... | collective-permute-start | bytes 733832 | tf_op jit(solution)/shard_map/ppermute | solution.py:27
  128.7 4.1 %collective-permute-start.8 = (bf16[4,2,112]{2,0,1:T(4,128)(2,1)S(1)}, bf16[4,2,112]{2,0,1:T(4,128)(2,1)S(1)}, u32[]{:S(2)}, u32[]{:S(2)}) collective-permute-start(bf16[4,2,112]{2,0,1:T(4,128)(2,1)S(1)} %fusion.78), channel_id=1, source_target_pairs={{0,128},{64,192},{128,0},{192,64},{256,384},{320,448},{384,256},{4... | collective-permute-start | bytes 5384 | tf_op jit(solution)/shard_map/ppermute | solution.py:27
  132.9 1.9 collective-permute-start.5
  134.8 3.8 %collective-permute-start.9 = (bf16[4,2,112]{2,0,1:T(4,128)(2,1)S(1)}, bf16[4,2,112]{2,0,1:T(4,128)(2,1)S(1)}, u32[]{:S(2)}, u32[]{:S(2)}) collective-permute-start(bf16[4,2,112]{2,0,1:T(4,128)(2,1)S(1)} %fusion.80), channel_id=1, source_target_pairs={{0,256},{64,320},{128,384},{192,448},{256,0},{320,64},{384,128},{4... | collective-permute-start | bytes 5384 | tf_op jit(solution)/shard_map/ppermute | solution.py:27
  138.7 3.6 %collective-permute-start.6 = (bf16[4,1,273]{2,0,1:T(4,128)(2,1)S(1)}, bf16[4,1,273]{2,0,1:T(4,128)(2,1)S(1)}, u32[]{:S(2)}, u32[]{:S(2)}) collective-permute-start(bf16[4,1,273]{2,0,1:T(4,128)(2,1)S(1)} %fusion.77), channel_id=1, source_target_pairs={{0,256},{64,320},{128,384},{192,448},{256,0},{320,64},{384,128},{4... | collective-permute-start | bytes 6560 | tf_op jit(solution)/shard_map/ppermute | solution.py:27
  142.3 3.9 %collective-permute-start.2 = (bf16[1,4,273,112]{3,2,1,0:T(8,128)(2,1)S(1)}, bf16[1,4,273,112]{3,2,1,0:T(8,128)(2,1)S(1)}, u32[]{:S(2)}, u32[]{:S(2)}) collective-permute-start(bf16[1,4,273,112]{3,2,1,0:T(8,128)(2,1)S(1)} %fusion.51), channel_id=1, source_target_pairs={{0,128},{64,192},{128,0},{192,64},{256,384},{320,448},{384,256},{4... | collective-permute-start | bytes 733832 | tf_op jit(solution)/shard_map/ppermute | solution.py:27
  146.3 0.6 gather_fusion.4
  146.8 0.7 select_convert_fusion
  147.5 4.8 %collective-permute-done.2 = bf16[1,4,273,112]{3,2,1,0:T(8,128)(2,1)S(1)} collective-permute-done((bf16[1,4,273,112]{3,2,1,0:T(8,128)(2,1)S(1)}, bf16[1,4,273,112]{3,2,1,0:T(8,128)(2,1)S(1)}, u32[]{:S(2)}, u32[]{:S(2)}) %collective-permute-start.2) | collective-permute-done | bytes 244640 | tf_op jit(solution)/shard_map/ppermute | solution.py:27
  152.3 0.1 fusion.33
  152.4 3.5 %collective-permute-start.3 = (bf16[1,4,273,112]{3,2,1,0:T(8,128)(2,1)S(1)}, bf16[1,4,273,112]{3,2,1,0:T(8,128)(2,1)S(1)}, u32[]{:S(2)}, u32[]{:S(2)}) collective-permute-start(bf16[1,4,273,112]{3,2,1,0:T(8,128)(2,1)S(1)} %fusion.33), channel_id=1, source_target_pairs={{0,256},{64,320},{128,384},{192,448},{256,0},{320,64},{384,128},{4... | collective-permute-start | bytes 733832 | tf_op jit(solution)/shard_map/ppermute | solution.py:27
  155.9 0.6 gather_fusion.3
  156.5 0.6 copy.27
  157.2 5.9 %collective-permute-done.3 = bf16[1,4,273,112]{3,2,1,0:T(8,128)(2,1)S(1)} collective-permute-done((bf16[1,4,273,112]{3,2,1,0:T(8,128)(2,1)S(1)}, bf16[1,4,273,112]{3,2,1,0:T(8,128)(2,1)S(1)}, u32[]{:S(2)}, u32[]{:S(2)}) %collective-permute-start.3) | collective-permute-done | bytes 244640 | tf_op jit(solution)/shard_map/ppermute | solution.py:27
  163.1 0.1 add_bitcast_fusion
  163.2 0.6 gather_fusion.1
  163.8 0.1 fusion.30
  163.9 1.4 copy.26
  165.3 28.3 %reduce-scatter.2.cloned.1.call-done = bf16[1,1024,112]{1,2,0:T(8,128)(2,1)} async-done(((bf16[16,1024,112]{1,2,0:T(8,128)(2,1)}), bf16[1,1024,112]{1,2,0:T(8,128)(2,1)}) %reduce-scatter.2.cloned.1.call-update) | async-done | bytes 229392 | tf_op jit(solution)/shard_map/reduce_scatter | solution.py:158
  (51 shorter events, 0.8 us)
Async XLA Ops:
  7.2 84.3 %copy-start = (bf16[1792,256]{1,0:T(8,128)(2,1)S(1)}, bf16[1792,256]{1,0:T(8,128)(2,1)}, u32[]{:S(2)}) copy-start(bf16[1792,256]{1,0:T(8,128)(2,1)} %param.9) | copy-start | bytes 2752516
  7.2 84.3 %all-gather.4.cloned.1.call-start = ((), (), s32[]{:S(2)}) async-start(), calls=%async_computation.1 | async-start | bytes 3899392 | tf_op jit(solution)/shard_map/all_gather | solution.py:79
  7.9 185.8 %reduce-scatter.2.cloned.1.call-start = ((), (), s32[]{:S(2)}) async-start(), calls=%async_computation.2 | async-start | bytes 3899392 | tf_op jit(solution)/shard_map/reduce_scatter | solution.py:158
  96.5 16.6 %collective-permute-start = (bf16[2,112]{0,1:T(8,128)(2,1)S(1)}, bf16[2,112]{0,1:T(8,128)(2,1)S(1)}, u32[]{:S(2)}, u32[]{:S(2)}) collective-permute-start(bf16[2,112]{0,1:T(8,128)(2,1)S(1)} %slice_bitcast_fusion.1), channel_id=1, source_target_pairs={{0,64},{64,128},{128,192},{192,256},{256,320},{320,384},{384,448},... | collective-permute-start | bytes 1352 | tf_op jit(solution)/shard_map/ppermute | solution.py:18
  111.9 1.3 copy-start.2
  111.9 1.3 copy-start.3
  116.3 0.7 copy-start.4
  116.3 0.7 copy-start.1
  116.3 1.5 copy-start.5
  118.7 10.0 %collective-permute-start.7 = (bf16[4,2,112]{2,0,1:T(4,128)(2,1)S(1)}, bf16[4,2,112]{2,0,1:T(4,128)(2,1)S(1)}, u32[]{:S(2)}, u32[]{:S(2)}) collective-permute-start(bf16[4,2,112]{2,0,1:T(4,128)(2,1)S(1)} %get-tuple-element.40), channel_id=1, source_target_pairs={{0,64},{64,0},{128,192},{192,128},{256,320},{320,256},{384,448},{4... | collective-permute-start | bytes 5384 | tf_op jit(solution)/shard_map/ppermute | solution.py:27
  121.8 11.1 %collective-permute-start.4 = (bf16[4,1,273]{2,0,1:T(4,128)(2,1)S(1)}, bf16[4,1,273]{2,0,1:T(4,128)(2,1)S(1)}, u32[]{:S(2)}, u32[]{:S(2)}) collective-permute-start(bf16[4,1,273]{2,0,1:T(4,128)(2,1)S(1)} %convert_bitcast_fusion.3), channel_id=1, source_target_pairs={{0,64},{64,0},{128,192},{192,128},{256,320},{320,256},{384,448},{4... | collective-permute-start | bytes 6560 | tf_op jit(solution)/shard_map/ppermute | solution.py:27
  126.4 15.8 %collective-permute-start.1 = (bf16[1,4,273,112]{3,2,1,0:T(8,128)(2,1)S(1)}, bf16[1,4,273,112]{3,2,1,0:T(8,128)(2,1)S(1)}, u32[]{:S(2)}, u32[]{:S(2)}) collective-permute-start(bf16[1,4,273,112]{3,2,1,0:T(8,128)(2,1)S(1)} %convert_bitcast_fusion), channel_id=1, source_target_pairs={{0,64},{64,0},{128,192},{192,128},{256,320},{320,256},{384,448},{4... | collective-permute-start | bytes 733832 | tf_op jit(solution)/shard_map/ppermute | solution.py:27
  128.7 6.1 %collective-permute-start.8 = (bf16[4,2,112]{2,0,1:T(4,128)(2,1)S(1)}, bf16[4,2,112]{2,0,1:T(4,128)(2,1)S(1)}, u32[]{:S(2)}, u32[]{:S(2)}) collective-permute-start(bf16[4,2,112]{2,0,1:T(4,128)(2,1)S(1)} %fusion.78), channel_id=1, source_target_pairs={{0,128},{64,192},{128,0},{192,64},{256,384},{320,448},{384,256},{4... | collective-permute-start | bytes 5384 | tf_op jit(solution)/shard_map/ppermute | solution.py:27
  132.9 5.7 %collective-permute-start.5 = (bf16[4,1,273]{2,0,1:T(4,128)(2,1)S(1)}, bf16[4,1,273]{2,0,1:T(4,128)(2,1)S(1)}, u32[]{:S(2)}, u32[]{:S(2)}) collective-permute-start(bf16[4,1,273]{2,0,1:T(4,128)(2,1)S(1)} %fusion.79), channel_id=1, source_target_pairs={{0,128},{64,192},{128,0},{192,64},{256,384},{320,448},{384,256},{4... | collective-permute-start | bytes 6560 | tf_op jit(solution)/shard_map/ppermute | solution.py:27
  134.8 11.4 %collective-permute-start.9 = (bf16[4,2,112]{2,0,1:T(4,128)(2,1)S(1)}, bf16[4,2,112]{2,0,1:T(4,128)(2,1)S(1)}, u32[]{:S(2)}, u32[]{:S(2)}) collective-permute-start(bf16[4,2,112]{2,0,1:T(4,128)(2,1)S(1)} %fusion.80), channel_id=1, source_target_pairs={{0,256},{64,320},{128,384},{192,448},{256,0},{320,64},{384,128},{4... | collective-permute-start | bytes 5384 | tf_op jit(solution)/shard_map/ppermute | solution.py:27
  138.7 17.2 %collective-permute-start.6 = (bf16[4,1,273]{2,0,1:T(4,128)(2,1)S(1)}, bf16[4,1,273]{2,0,1:T(4,128)(2,1)S(1)}, u32[]{:S(2)}, u32[]{:S(2)}) collective-permute-start(bf16[4,1,273]{2,0,1:T(4,128)(2,1)S(1)} %fusion.77), channel_id=1, source_target_pairs={{0,256},{64,320},{128,384},{192,448},{256,0},{320,64},{384,128},{4... | collective-permute-start | bytes 6560 | tf_op jit(solution)/shard_map/ppermute | solution.py:27
  142.3 10.0 %collective-permute-start.2 = (bf16[1,4,273,112]{3,2,1,0:T(8,128)(2,1)S(1)}, bf16[1,4,273,112]{3,2,1,0:T(8,128)(2,1)S(1)}, u32[]{:S(2)}, u32[]{:S(2)}) collective-permute-start(bf16[1,4,273,112]{3,2,1,0:T(8,128)(2,1)S(1)} %fusion.51), channel_id=1, source_target_pairs={{0,128},{64,192},{128,0},{192,64},{256,384},{320,448},{384,256},{4... | collective-permute-start | bytes 733832 | tf_op jit(solution)/shard_map/ppermute | solution.py:27
  152.4 10.7 %collective-permute-start.3 = (bf16[1,4,273,112]{3,2,1,0:T(8,128)(2,1)S(1)}, bf16[1,4,273,112]{3,2,1,0:T(8,128)(2,1)S(1)}, u32[]{:S(2)}, u32[]{:S(2)}) collective-permute-start(bf16[1,4,273,112]{3,2,1,0:T(8,128)(2,1)S(1)} %fusion.33), channel_id=1, source_target_pairs={{0,256},{64,320},{128,384},{192,448},{256,0},{320,64},{384,128},{4... | collective-permute-start | bytes 733832 | tf_op jit(solution)/shard_map/ppermute | solution.py:27
Sparse Core Ops, SparseCore 0:
  10.1 81.3 all-gather.3
  116.5 77.1 reduce-scatter.1
where the time goes:
time: 201 us
  waiting for transfers between devices  117 us (58%)
  starting transfers between devices  29.5 us (15%)
  between operations  14.5 us (7%)
  matrix products  13.4 us (7%)
  blocking collectives  12.1 us (6%)
  local copies, waits for them, and re-layouts  7.13 us (4%)
  other arithmetic  6.52 us (3%)
    all_gather x1, waiting for transfers between devices, local(): lax.all_gather(tokens, 'tp', axis=1, tiled=True)  77.7 us
    reduce_scatter x1, waiting for transfers between devices, local(): summed = lax.psum_scatter(product, 'tp', scatter_dimension=0, tiled=True)  28.3 us
    ppermute x9, starting transfers between devices, psum_doubling(): lax.ppermute(tuple((t.astype(jnp.bfloat16) for t in total)), axis, pairs)  27.5 us
    all_gather x1, blocking collectives, local(): lax.all_gather(tail_state.astype(jnp.bfloat16), 'seq').astype(jnp.float32)  12.1 us
    ppermute x9, waiting for transfers between devices, psum_doubling(): lax.ppermute(tuple((t.astype(jnp.bfloat16) for t in total)), axis, pairs)  10.7 us
  transfers between devices with their start and end apart: 12, of which 4 were waited for; matrix products, arithmetic and copies ran while one was open for 9% of the time, Pallas kernels for 0%

commit v1 on v0

--- a/solution.py
+++ b/solution.py
@@ -76,7 +76,11 @@
     positions = first_row + jnp.arange(tok_rows, dtype=jnp.int32)
     seg = segment_ids(positions, ends)
     proj = jnp.dot(
-        lax.all_gather(tokens, "tp", axis=1, tiled=True), w_in, preferred_element_type=jnp.float32
+        jnp.concatenate(
+            lax.all_to_all(jnp.stack([tokens] * lax.axis_size("tp")), "tp", 0, 0), axis=1
+        ),
+        w_in,
+        preferred_element_type=jnp.float32,
     )
     proj = proj.astype(jnp.bfloat16).reshape(tok_rows, local_heads, width)
     gate_pre = proj[:, :, 2 * FEAT + HD :].reshape(tok_rows, local_cols)

time: 201 us -> 301 us (1.50)
  the two profiles are of different devices: /device:TPU:4 before, /device:TPU:20 now
where the time goes in v1:
time: 301 us; the launch traced here: 300 us
  waiting for transfers between devices  200 us (66%)
  starting transfers between devices  44.1 us (15%)
  between operations  14.4 us (5%)
  matrix products  14.3 us (5%)
  blocking collectives  12 us (4%)
  local copies, waits for them, and re-layouts  10.5 us (3%)
  other arithmetic  5.18 us (2%)
    all_to_all x1, waiting for transfers between devices, local(): lax.all_to_all(jnp.stack([tokens] * lax.axis_size('tp')), 'tp', 0, 0)  156 us
    reduce_scatter x1, waiting for transfers between devices, local(): summed = lax.psum_scatter(product, 'tp', scatter_dimension=0, tiled=True)  30.1 us
    ppermute x9, starting transfers between devices, psum_doubling(): lax.ppermute(tuple((t.astype(jnp.bfloat16) for t in total)), axis, pairs)  26.4 us
    all_to_all x1, starting transfers between devices, local(): lax.all_to_all(jnp.stack([tokens] * lax.axis_size('tp')), 'tp', 0, 0)  15.4 us
    all_gather x1, blocking collectives, local(): lax.all_gather(tail_state.astype(jnp.bfloat16), 'seq').astype(jnp.float32)  12 us
    ppermute x9, waiting for transfers between devices, psum_doubling(): lax.ppermute(tuple((t.astype(jnp.bfloat16) for t in total)), axis, pairs)  11.9 us
  transfers between devices with their start and end apart: 12, of which 6 were waited for; matrix products, arithmetic and copies ran while one was open for 5% of the time, Pallas kernels for 0%

profile of v1, /device:TPU:20, one launch (start us, length us, event | category | flops | bytes accessed | tf_op | source)
XLA Modules:
  0.0 300.1 jit_solution(6153945361135634518)
XLA Ops:
  7.2 3.3 %stack.2 = bf16[16,1024,112]{1,2,0:T(8,128)(2,1)} broadcast(bf16[1024,112]{0,1:T(8,128)(2,1)} %param.8), dimensions={1,2} | broadcast | bytes 3899392 | tf_op jit(solution)/shard_map/stack | solution.py:80
  10.5 15.4 %all-to-all-start = ((bf16[16,1024,112]{1,2,0:T(8,128)(2,1)}), bf16[16,1024,112]{1,2,0:T(8,128)(2,1)}, u32[]{:S(2)}, u32[]{:S(2)}) async-start(bf16[16,1024,112]{1,2,0:T(8,128)(2,1)} %stack.2), calls=%async_computation | async-start | bytes 7340032 | tf_op jit(solution)/shard_map/all_to_all | solution.py:80
  25.9 0.2 reduce-window.7
  26.2 0.6 dynamic_slice.6
  27.0 0.6 bitcast_subtract_fusion
  27.6 0.6 and_convert_fusion.1
  28.3 1.4 fusion.74
  29.7 156.1 %all-to-all-done = bf16[16,1024,112]{1,2,0:T(8,128)(2,1)} async-done(((bf16[16,1024,112]{1,2,0:T(8,128)(2,1)}), bf16[16,1024,112]{1,2,0:T(8,128)(2,1)}, u32[]{:S(2)}, u32[]{:S(2)}) %all-to-all-start) | async-done | bytes 3670048 | tf_op jit(solution)/shard_map/all_to_all | solution.py:80
  185.7 3.2 %fusion.8 = bf16[1024,1,256]{0,2,1:T(8,128)(2,1)S(1)} fusion(bf16[1024,1792]{0,1:T(8,128)(2,1)} %bitcast.1, bf16[1792,256]{1,0:T(8,128)(2,1)S(1)} %copy-done), kind=kOutput, calls=%fused_computation.15 | convolution fusion | flops 939786240 | bytes 5111808 | tf_op jit(solution)/shard_map/dot_general | solution.py:78
  189.0 1.7 fusion.9
  190.8 0.1 multiply_multiply_fusion.2
  190.9 1.8 fusion.25
  192.7 12.0 %all-gather.1 = bf16[8,273,112]{2,1,0:T(8,128)(2,1)S(1)} all-gather(bf16[1,273,112]{2,1,0:T(8,128)(2,1)S(1)} %fusion.25), channel_id=2, replica_groups=mesh['seq'=8,'tp'=16,'req'=4] {'seq'}, dimensions={0}, use_global_device_ids=true | all-gather | bytes 550368 | tf_op jit(solution)/shard_map/all_gather | solution.py:141
  204.7 0.1 multiply_multiply_fusion.1
  204.8 2.3 collective-permute-start
  207.1 0.2 fusion.21
  207.3 1.2 multiply_reduce_fusion
  208.6 1.5 collective-permute-done
  210.0 3.2 %fusion.38 = bf16[1024,1792]{0,1} fusion(bf16[112,1792]{1,0:T(8,128)(2,1)S(1)} %copy-done.2, bf16[1024,112]{0,1:T(8,128)(2,1)S(1)} %slice_bitcast_fusion, f32[1,112,1024]{2,1,0:T(8,128)S(1)} %get-tuple-element.39, bf16[2,112]{0,1:T(8,128)(2,1)S(1)} %collective-permute-done, f32[1024]{0:T(1024)S(1)} %get-tuple-element.28, f32[112]{0:T(128)S(1)} %get-tuple-element.33, ...), kind=kOutput, calls=%fused_computation.57 | convolution fusion | flops 413908992 | bytes 4778176
  213.2 0.6 copy-done.7
  213.9 0.6 gather_fusion
  214.7 0.6 gather_fusion.2
  215.4 0.2 maximum_bitcast_fusion.2
  215.5 0.9 copy-done.4
  216.4 2.3 fusion
  218.8 2.7 collective-permute-start.1
  221.4 0.2 fusion.91
  221.6 1.9 collective-permute-start.7
  223.6 0.8 fusion.65
  224.3 2.4 collective-permute-start.4
  226.8 3.6 %collective-permute-start.8 = (bf16[4,2,112]{2,0,1:T(4,128)(2,1)S(1)}, bf16[4,2,112]{2,0,1:T(4,128)(2,1)S(1)}, u32[]{:S(2)}, u32[]{:S(2)}) collective-permute-start(bf16[4,2,112]{2,0,1:T(4,128)(2,1)S(1)} %fusion.78), channel_id=1, source_target_pairs={{0,128},{64,192},{128,0},{192,64},{256,384},{320,448},{384,256},{4... | collective-permute-start | bytes 5384 | tf_op jit(solution)/shard_map/ppermute | solution.py:27
  230.4 2.3 collective-permute-start.5
  232.7 2.8 collective-permute-start.9
  235.5 0.4 collective-permute-done.5
  235.9 4.2 %collective-permute-start.6 = (bf16[4,1,273]{2,0,1:T(4,128)(2,1)S(1)}, bf16[4,1,273]{2,0,1:T(4,128)(2,1)S(1)}, u32[]{:S(2)}, u32[]{:S(2)}) collective-permute-start(bf16[4,1,273]{2,0,1:T(4,128)(2,1)S(1)} %fusion.77), channel_id=1, source_target_pairs={{0,256},{64,320},{128,384},{192,448},{256,0},{320,64},{384,128},{4... | collective-permute-start | bytes 6560 | tf_op jit(solution)/shard_map/ppermute | solution.py:27
  240.2 3.6 %collective-permute-start.2 = (bf16[1,4,273,112]{3,2,1,0:T(8,128)(2,1)S(1)}, bf16[1,4,273,112]{3,2,1,0:T(8,128)(2,1)S(1)}, u32[]{:S(2)}, u32[]{:S(2)}) collective-permute-start(bf16[1,4,273,112]{3,2,1,0:T(8,128)(2,1)S(1)} %fusion.51), channel_id=1, source_target_pairs={{0,128},{64,192},{128,0},{192,64},{256,384},{320,448},{384,256},{4... | collective-permute-start | bytes 733832 | tf_op jit(solution)/shard_map/ppermute | solution.py:27
  243.8 0.6 gather_fusion.4
  244.4 0.7 select_convert_fusion
  245.0 5.1 %collective-permute-done.2 = bf16[1,4,273,112]{3,2,1,0:T(8,128)(2,1)S(1)} collective-permute-done((bf16[1,4,273,112]{3,2,1,0:T(8,128)(2,1)S(1)}, bf16[1,4,273,112]{3,2,1,0:T(8,128)(2,1)S(1)}, u32[]{:S(2)}, u32[]{:S(2)}) %collective-permute-start.2) | collective-permute-done | bytes 244640 | tf_op jit(solution)/shard_map/ppermute | solution.py:27
  250.2 3.0 %collective-permute-start.3 = (bf16[1,4,273,112]{3,2,1,0:T(8,128)(2,1)S(1)}, bf16[1,4,273,112]{3,2,1,0:T(8,128)(2,1)S(1)}, u32[]{:S(2)}, u32[]{:S(2)}) collective-permute-start(bf16[1,4,273,112]{3,2,1,0:T(8,128)(2,1)S(1)} %fusion.33), channel_id=1, source_target_pairs={{0,256},{64,320},{128,384},{192,448},{256,0},{320,64},{384,128},{4... | collective-permute-start | bytes 733832 | tf_op jit(solution)/shard_map/ppermute | solution.py:27
  253.3 0.6 gather_fusion.3
  253.9 0.6 copy.28
  254.5 6.4 %collective-permute-done.3 = bf16[1,4,273,112]{3,2,1,0:T(8,128)(2,1)S(1)} collective-permute-done((bf16[1,4,273,112]{3,2,1,0:T(8,128)(2,1)S(1)}, bf16[1,4,273,112]{3,2,1,0:T(8,128)(2,1)S(1)}, u32[]{:S(2)}, u32[]{:S(2)}) %collective-permute-start.3) | collective-permute-done | bytes 244640 | tf_op jit(solution)/shard_map/ppermute | solution.py:27
  260.9 0.1 add_bitcast_fusion
  261.0 0.6 gather_fusion.1
  261.6 0.1 fusion.30
  261.7 1.4 copy.27
  263.1 30.1 %reduce-scatter.2.cloned.1.call-done = bf16[1,1024,112]{1,2,0:T(8,128)(2,1)} async-done(((bf16[16,1024,112]{1,2,0:T(8,128)(2,1)}), bf16[1,1024,112]{1,2,0:T(8,128)(2,1)}) %reduce-scatter.2.cloned.1.call-update) | async-done | bytes 229392 | tf_op jit(solution)/shard_map/reduce_scatter | solution.py:162
  (57 shorter events, 1.1 us)
Async XLA Ops:
  7.2 178.6 %copy-start = (bf16[1792,256]{1,0:T(8,128)(2,1)S(1)}, bf16[1792,256]{1,0:T(8,128)(2,1)}, u32[]{:S(2)}) copy-start(bf16[1792,256]{1,0:T(8,128)(2,1)} %param.9) | copy-start | bytes 2752516
  10.5 15.4 %copy-start.8 = (s32[4]{0:T(128)S(1)}, s32[4]{0:T(128)}, u32[]{:S(2)}) copy-start(s32[4]{0:T(128)} %param.13) | copy-start | bytes 52
  10.5 17.8 %copy-start.5 = (f32[3,112]{1,0:T(4,128)S(1)}, f32[3,112]{1,0:T(4,128)}, u32[]{:S(2)}) copy-start(f32[3,112]{1,0:T(4,128)} %param.10) | copy-start | bytes 4036
  10.5 175.2 %all-to-all-start = ((bf16[16,1024,112]{1,2,0:T(8,128)(2,1)}), bf16[16,1024,112]{1,2,0:T(8,128)(2,1)}, u32[]{:S(2)}, u32[]{:S(2)}) async-start(bf16[16,1024,112]{1,2,0:T(8,128)(2,1)} %stack.2), calls=%async_computation | async-start | bytes 7340032 | tf_op jit(solution)/shard_map/all_to_all | solution.py:80
  25.9 267.4 %reduce-scatter.2.cloned.1.call-start = ((), (), s32[]{:S(2)}) async-start(), calls=%async_computation.2 | async-start | bytes 3899392 | tf_op jit(solution)/shard_map/reduce_scatter | solution.py:162
  188.9 1.8 copy-start.3
  204.8 5.2 %collective-permute-start = (bf16[2,112]{0,1:T(8,128)(2,1)S(1)}, bf16[2,112]{0,1:T(8,128)(2,1)S(1)}, u32[]{:S(2)}, u32[]{:S(2)}) collective-permute-start(bf16[2,112]{0,1:T(8,128)(2,1)S(1)} %slice_bitcast_fusion.1), channel_id=1, source_target_pairs={{0,64},{64,128},{128,192},{192,256},{256,320},{320,384},{384,448},... | collective-permute-start | bytes 1352 | tf_op jit(solution)/shard_map/ppermute | solution.py:18
  207.3 2.7 copy-start.2
  207.3 2.7 copy-start.6
  213.2 0.7 copy-start.7
  213.2 0.7 copy-start.1
  215.3 1.0 copy-start.4
  218.8 21.3 %collective-permute-start.1 = (bf16[1,4,273,112]{3,2,1,0:T(8,128)(2,1)S(1)}, bf16[1,4,273,112]{3,2,1,0:T(8,128)(2,1)S(1)}, u32[]{:S(2)}, u32[]{:S(2)}) collective-permute-start(bf16[1,4,273,112]{3,2,1,0:T(8,128)(2,1)S(1)} %convert_bitcast_fusion), channel_id=1, source_target_pairs={{0,64},{64,0},{128,192},{192,128},{256,320},{320,256},{384,448},{4... | collective-permute-start | bytes 733832 | tf_op jit(solution)/shard_map/ppermute | solution.py:27
  221.6 5.2 %collective-permute-start.7 = (bf16[4,2,112]{2,0,1:T(4,128)(2,1)S(1)}, bf16[4,2,112]{2,0,1:T(4,128)(2,1)S(1)}, u32[]{:S(2)}, u32[]{:S(2)}) collective-permute-start(bf16[4,2,112]{2,0,1:T(4,128)(2,1)S(1)} %get-tuple-element.40), channel_id=1, source_target_pairs={{0,64},{64,0},{128,192},{192,128},{256,320},{320,256},{384,448},{4... | collective-permute-start | bytes 5384 | tf_op jit(solution)/shard_map/ppermute | solution.py:27
  224.3 6.0 %collective-permute-start.4 = (bf16[4,1,273]{2,0,1:T(4,128)(2,1)S(1)}, bf16[4,1,273]{2,0,1:T(4,128)(2,1)S(1)}, u32[]{:S(2)}, u32[]{:S(2)}) collective-permute-start(bf16[4,1,273]{2,0,1:T(4,128)(2,1)S(1)} %convert_bitcast_fusion.3), channel_id=1, source_target_pairs={{0,64},{64,0},{128,192},{192,128},{256,320},{320,256},{384,448},{4... | collective-permute-start | bytes 6560 | tf_op jit(solution)/shard_map/ppermute | solution.py:27
  226.8 5.9 %collective-permute-start.8 = (bf16[4,2,112]{2,0,1:T(4,128)(2,1)S(1)}, bf16[4,2,112]{2,0,1:T(4,128)(2,1)S(1)}, u32[]{:S(2)}, u32[]{:S(2)}) collective-permute-start(bf16[4,2,112]{2,0,1:T(4,128)(2,1)S(1)} %fusion.78), channel_id=1, source_target_pairs={{0,128},{64,192},{128,0},{192,64},{256,384},{320,448},{384,256},{4... | collective-permute-start | bytes 5384 | tf_op jit(solution)/shard_map/ppermute | solution.py:27
  230.4 5.5 %collective-permute-start.5 = (bf16[4,1,273]{2,0,1:T(4,128)(2,1)S(1)}, bf16[4,1,273]{2,0,1:T(4,128)(2,1)S(1)}, u32[]{:S(2)}, u32[]{:S(2)}) collective-permute-start(bf16[4,1,273]{2,0,1:T(4,128)(2,1)S(1)} %fusion.79), channel_id=1, source_target_pairs={{0,128},{64,192},{128,0},{192,64},{256,384},{320,448},{384,256},{4... | collective-permute-start | bytes 6560 | tf_op jit(solution)/shard_map/ppermute | solution.py:27
  232.7 11.0 %collective-permute-start.9 = (bf16[4,2,112]{2,0,1:T(4,128)(2,1)S(1)}, bf16[4,2,112]{2,0,1:T(4,128)(2,1)S(1)}, u32[]{:S(2)}, u32[]{:S(2)}) collective-permute-start(bf16[4,2,112]{2,0,1:T(4,128)(2,1)S(1)} %fusion.80), channel_id=1, source_target_pairs={{0,256},{64,320},{128,384},{192,448},{256,0},{320,64},{384,128},{4... | collective-permute-start | bytes 5384 | tf_op jit(solution)/shard_map/ppermute | solution.py:27
  235.9 17.4 %collective-permute-start.6 = (bf16[4,1,273]{2,0,1:T(4,128)(2,1)S(1)}, bf16[4,1,273]{2,0,1:T(4,128)(2,1)S(1)}, u32[]{:S(2)}, u32[]{:S(2)}) collective-permute-start(bf16[4,1,273]{2,0,1:T(4,128)(2,1)S(1)} %fusion.77), channel_id=1, source_target_pairs={{0,256},{64,320},{128,384},{192,448},{256,0},{320,64},{384,128},{4... | collective-permute-start | bytes 6560 | tf_op jit(solution)/shard_map/ppermute | solution.py:27
  240.2 9.9 %collective-permute-start.2 = (bf16[1,4,273,112]{3,2,1,0:T(8,128)(2,1)S(1)}, bf16[1,4,273,112]{3,2,1,0:T(8,128)(2,1)S(1)}, u32[]{:S(2)}, u32[]{:S(2)}) collective-permute-start(bf16[1,4,273,112]{3,2,1,0:T(8,128)(2,1)S(1)} %fusion.51), channel_id=1, source_target_pairs={{0,128},{64,192},{128,0},{192,64},{256,384},{320,448},{384,256},{4... | collective-permute-start | bytes 733832 | tf_op jit(solution)/shard_map/ppermute | solution.py:27
  250.2 10.7 %collective-permute-start.3 = (bf16[1,4,273,112]{3,2,1,0:T(8,128)(2,1)S(1)}, bf16[1,4,273,112]{3,2,1,0:T(8,128)(2,1)S(1)}, u32[]{:S(2)}, u32[]{:S(2)}) collective-permute-start(bf16[1,4,273,112]{3,2,1,0:T(8,128)(2,1)S(1)} %fusion.33), channel_id=1, source_target_pairs={{0,256},{64,320},{128,384},{192,448},{256,0},{320,64},{384,128},{4... | collective-permute-start | bytes 733832 | tf_op jit(solution)/shard_map/ppermute | solution.py:27
Sparse Core Ops, SparseCore 0:
  213.3 79.8 reduce-scatter.1
